TPU v7x, 128 devices: a whole 4x4x4 slice. The times are simulated.
128 devices in a mesh: feed: 8 (over y, core), chan: 16 (over z, x).
Axes of the slice: x: 4, y: 4, z: 4, core: 2. Of those that a mesh axis runs over, the one named last changes fastest.
Arguments:
- voltages: bfloat16 [2, 2, 16, 8192, 1024], P(None, None, 'chan', None, 'feed'), may hold values from -6 to 6
- history: bfloat16 [2, 2, 16, 48, 1024], P(None, None, 'chan', None, 'feed'), may hold values from -6 to 6
- gains: float32 [2, 2, 16, 1024], P(None, None, 'chan', 'feed'), may hold values from -4 to 4
- weights: bfloat16 [2, 16, 1024, 1024], P(None, 'chan'), may hold values from -0.09375 to 0.09375
- beam_lists: int32 [16, 128], replicated, may hold values from 0 to 1023, as said below
- beam_counts: int32 [16], replicated, may hold values from 1 to 128, as said below
Outputs:
- power_blocks: bfloat16 [256, 256, 2048], P('feed', None, 'chan')
Inputs may be any that keep to these rules, and one draw needn't show every extreme that they name: `beam_lists`: row n holds in its first beam_counts[n] entries, in increasing order, the beams that node n owns, and 0 in the others; every beam is owned by exactly one node. `beam_counts`: the counts sum to 1024; some node owns exactly 128 beams.
All inputs are finite; a program needn't handle non-finite values.
Results may differ from a plain program's by a relative error of at most 0.013.
Values may be sent and summed in bfloat16 or wider, within the bound.
No kernel may reach another device: no remote copies, remote signals or barrier semaphores. Data moves between devices by JAX's collectives and lax.ppermute only.
A program may use at most 192 MiB of HBM per device.

v0:
```python
import math
import jax
import jax.numpy as jnp
from jax import lax
from jax.sharding import PartitionSpec as P

U = 16
TAPS = 4
TINT = 2


def window_taps():
    length = TAPS * U
    positions = jnp.arange(length, dtype=jnp.float32)
    offsets = (positions - (length - 1) / 2.0) / U
    hann_taper = 0.5 - 0.5 * jnp.cos(2.0 * math.pi * (positions + 0.5) / length)
    taps_window = jnp.sinc(offsets) * hann_taper
    return taps_window / jnp.sqrt(jnp.sum(taps_window * taps_window) / U)


def dft_table():
    index_n = jnp.arange(U, dtype=jnp.int32)
    products = index_n[:, None] * index_n[None, :] % U
    phases = 2.0 * math.pi * products.astype(jnp.float32) / U
    cosine = jnp.cos(phases) / math.sqrt(U)
    sine = jnp.sin(phases) / math.sqrt(U)
    return jnp.stack([jnp.stack([cosine, -sine]), jnp.stack([sine, cosine])])


def filterbank(stream, frames, gains):
    shape_in = stream.shape
    taps_window = window_taps().reshape(TAPS, U)
    table = dft_table()
    frames_data = stream.reshape(
        shape_in[0], shape_in[1], shape_in[2], frames + TAPS - 1, U, shape_in[4]
    )
    filtered = taps_window[0][:, None] * frames_data[:, :, :, 0:frames].astype(jnp.float32)
    for tap_index in range(1, TAPS):
        filtered = filtered + taps_window[tap_index][:, None] * frames_data[
            :, :, :, tap_index : tap_index + frames
        ].astype(jnp.float32)
    spec_parts = []
    for part_out in range(2):
        total = None
        for part_in in range(2):
            for index_n in range(U):
                term = (
                    filtered[part_in, :, :, :, index_n : index_n + 1, :]
                    * table[part_in, part_out, index_n][:, None]
                )
                total = term if total is None else total + term
        spec_parts.append(total)
    gain_cols = gains[:, :, :, None, None, :]
    real_part = gain_cols[0] * spec_parts[0] - gain_cols[1] * spec_parts[1]
    imag_part = gain_cols[0] * spec_parts[1] + gain_cols[1] * spec_parts[0]
    return jnp.stack([real_part, imag_part]).astype(jnp.bfloat16)


def detect(calibrated, weights):
    spectra_here = calibrated.shape[3]
    fine_items = calibrated.shape[4]
    beam_total = weights.shape[3]
    rows_real = calibrated[0, :, 0].reshape(-1, calibrated.shape[5])
    rows_imag = calibrated[1, :, 0].reshape(-1, calibrated.shape[5])
    weight_real = weights[0, 0]
    weight_imag = weights[1, 0]
    upper_block = jnp.concatenate([weight_real, weight_imag], axis=1)
    lower_block = jnp.concatenate([-weight_imag, weight_real], axis=1)
    joined = jnp.dot(rows_real, upper_block, preferred_element_type=jnp.float32) + jnp.dot(
        rows_imag, lower_block, preferred_element_type=jnp.float32
    )
    real_part = joined[:, :beam_total]
    imag_part = joined[:, beam_total:]
    power_sum = (real_part * real_part + imag_part * imag_part).reshape(
        2, spectra_here, fine_items, beam_total
    )
    power_sum = jnp.sum(power_sum, axis=0).reshape(
        spectra_here // TINT, TINT, fine_items, beam_total
    )
    power_sum = jnp.sum(power_sum, axis=1) * (1.0 / (4.0 * TINT))
    outputs = [power_sum.astype(jnp.bfloat16)]
    return jnp.stack(outputs, axis=1)


def on_device(voltages, history, gains, weights, beam_lists, beam_counts):
    capacity = beam_lists.shape[1]
    flat_ids = beam_lists.reshape(-1)
    live_slots = (jnp.arange(capacity, dtype=jnp.int32)[None, :] < beam_counts[:, None]).reshape(-1)
    stream = jnp.concatenate([history, voltages], axis=3)
    calibrated = filterbank(stream, voltages.shape[3] // U, gains)
    beam_calibrated = lax.all_to_all(calibrated, "feed", split_axis=3, concat_axis=5, tiled=True)
    detected = detect(beam_calibrated, weights)
    bins_local, coarse_local, fine_items, beam_total = detected.shape
    picked = jnp.take(
        detected.reshape(bins_local, coarse_local * fine_items, beam_total), flat_ids, axis=2
    )
    return lax.all_to_all(
        jnp.where(live_slots, picked, jnp.zeros((), jnp.bfloat16)),
        "chan",
        split_axis=2,
        concat_axis=1,
        tiled=True,
    )


def solution(mesh):
    in_specs = (
        P(None, None, "chan", None, "feed"),
        P(None, None, "chan", None, "feed"),
        P(None, None, "chan", "feed"),
        P(None, "chan", None, None),
        P(),
        P(),
    )
    out_specs = P("feed", None, "chan")
    return jax.shard_map(
        on_device, mesh=mesh, in_specs=in_specs, out_specs=out_specs, check_vma=False
    )
```

profile of v0, /device:TPU:0, one launch (start us, length us, event | category | flops | bytes accessed | tf_op | source)
XLA Modules:
  0.0 429.2 jit_solution(4782768966015367416)
XLA Ops:
  5.0 11.6 %fusion.35 = (bf16[2,2,1,512,16,128]{5,4,3,1,0,2:T(8,128)(2,1)}, bf16[2,2,1,512,16,128]{5,4,3,1,0,2:T(8,128)(2,1)}, bf16[2,2,1,512,16,128]{5,4,3,1,0,2:T(8,128)(2,1)}, bf16[2,2,1,512,16,128]{5,4,3,1,0,2:T(8,128)(2,1)}) fusion(bf16[2,2,1,515,16,128]{5,4,3,1,0,2:T(8,128)(2,1)S(1)} %bitcast.249), kind=kLoop, calls=%fused_computation.172 | loop fusion | bytes 67108864 | tf_op jit(solution)/shard_map/slice | solution.py:37
  17.4 56.0 %multiply_add_fusion = f32[2,2,1,512,16,128]{5,1,3,4,2,0:T(2,128)} fusion(f32[16]{0:T(128)S(1)} %get-tuple-element.117, f32[16]{0:T(128)S(1)} %get-tuple-element.118, f32[16]{0:T(128)S(1)} %get-tuple-element.119, f32[16]{0:T(128)S(1)} %get-tuple-element.116, bf16[2,2,1,512,16,128]{5,4,3,1,0,2:T(8,128)(2,1)} %get-tuple-element.43, ...), kind=kLoop, calls=%fused_computation.1 | loop fusion | flops 46137344 | bytes 50331904 | tf_op jit(solution)/shard_map/add | solution.py:39
  73.3 6.9 %slice_bitcast_fusion.33 = (f32[2,512,128]{2,0,1:T(2,128)S(1)}, f32[2,512,128]{2,0,1:T(2,128)S(1)}, f32[2,512,128]{2,0,1:T(2,128)S(1)}, f32[2,512,128]{2,0,1:T(2...) fusion(f32[2,2,1,512,16,128]{5,1,3,4,2,0:T(2,128)} %multiply_ad, ...), kind=kLoop, calls=%fused_computation.61 | loop fusion | bytes 19922944 | tf_op jit(solution)/shard_map/mul | solution.py:48
  80.2 4.9 %slice_bitcast_fusion.32 = (f32[2,512,128]{2,0,1:T(2,128)}, f32[2,512,128]{2,0,1:T(2,128)}, f32[2,512,128]{2,0,1:T(2,128)}, f32[2,512,128]{2,0,1:T(2,128)}, f32[...) fusion(f32[2,2,1,512,16,128]{5,1,3,4,2,0:T(2,128)} %multiply_ad, ...), kind=kLoop, calls=%fused_computation.60 | loop fusion | bytes 13631488 | tf_op jit(solution)/shard_map/mul | solution.py:48
  85.4 49.3 %fusion.1 = (bf16[1,2,1,512,16,128]{5,4,1,0,2,3:T(8,128)(2,1)}, f32[1,2,512,16,128]{4,3,1,2,0:T(8,128)}, f32[1,2,512,16,128]{4,3,1,2,0:T(8,128)}) fusion(f32[2,128]{1,0:T(2,128)S(1)} %bitcast.259, f32[2,128]{1,0:T(2,128)S(1)} %bitcast.257, f32[16]{0:T(128)S(1)} %get-tuple-element.81, f32[2,512,128]{2,0,1:T(2,128)S(1)} %get-tuple-element.9, ...), kind=kLoop, calls=%fused_computation.13 | loop fusion | flops 272629760 | bytes 37754880 | tf_op jit(solution)/shard_map/stack | solution.py:56
  134.7 7.9 %fusion.2 = bf16[1,2,1,512,16,128]{5,4,1,0,2,3:T(8,128)(2,1)S(1)} fusion(f32[1,2,512,16,128]{4,3,1,2,0:T(8,128)} %get-tuple-element.7, f32[1,2,512,16,128]{4,3,1,2,0:T(8,128)} %get-tuple-element.6, f32[2,128]{1,0:T(2,128)S(1)} %bitcast.260, f32[2,128]{1,0:T(2,128)S(1)} %bitcast.258), kind=kLoop, calls=%fused_computation.14 | loop fusion | flops 8388608 | bytes 20973568 | tf_op jit(solution)/shard_map/stack | solution.py:56
  142.6 6.5 %pad_maximum_fusion.1 = bf16[2,2,1,512,16,128]{5,4,1,0,2,3:T(8,128)(2,1)} fusion(bf16[1,2,1,512,16,128]{5,4,1,0,2,3:T(8,128)(2,1)S(1)} %fusion.2, bf16[1,2,1,512,16,128]{5,4,1,0,2,3:T(8,128)(2,1)} %get-tuple-element.5), kind=kLoop, calls=%fused_computation.6 | loop fusion | flops 4194304 | bytes 16777216 | tf_op jit(solution)/shard_map/stack | solution.py:56
  149.1 5.1 %all-to-all-start = ((bf16[2,2,1,512,16,128]{5,4,1,0,2,3:T(8,128)(2,1)}), bf16[2,2,1,512,16,128]{5,4,1,0,2,3:T(8,128)(2,1)}, u32[]{:S(2)}, u32[]{:S(2)}) async-start(bf16[2,2,1,512,16,128]{5,4,1,0,2,3:T(8,128)(2,1)} %pad_maximum_fusion.1), calls=%async_computation | async-start | bytes 16777216 | tf_op jit(solution)/shard_map/all_to_all | solution.py:91
  156.0 4.7 %slice_bitcast_fusion.1 = (bf16[1024,1024]{1,0:T(8,128)(2,1)}, bf16[1024,1024]{1,0:T(8,128)(2,1)}) fusion(bf16[2,1,1024,1024]{3,2,1,0:T(8,128)(2,1)} %param.9), kind=kLoop, calls=%fused_computation.29 | loop fusion | bytes 8388608 | tf_op jit(solution)/shard_map/squeeze | solution.py:65
  160.7 88.1 %all-to-all-done = bf16[2,2,1,512,16,128]{5,4,1,0,2,3:T(8,128)(2,1)} async-done(((bf16[2,2,1,512,16,128]{5,4,1,0,2,3:T(8,128)(2,1)}), bf16[2,2,1,512,16,128]{5,4,1,0,2,3:T(8,128)(2,1)}, u32[]{:S(2)}, u32[]{:S(2)}) %all-to-all-start) | async-done | bytes 8388640 | tf_op jit(solution)/shard_map/all_to_all | solution.py:91
  248.8 8.1 %copy.43 = bf16[2,2,1,512,16,128]{5,4,3,1,0,2:T(8,128)(2,1)} copy(bf16[2,2,1,512,16,128]{5,4,1,0,2,3:T(8,128)(2,1)} %all-to-all-done) | data formatting | bytes 16777216 | tf_op jit(solution)/shard_map/all_to_all | solution.py:91
  261.2 4.9 %copy.44 = bf16[1,2,1,64,16,8,128]{6,5,4,3,1,2,0:T(8,128)(2,1)S(1)} copy(bf16[1,2,1,64,16,8,128]{6,4,3,5,1,0,2:T(8,128)(2,1)S(1)} %get-tuple-element.45) | data formatting | bytes 8388608 | tf_op jit(solution)/shard_map/slice | solution.py:63
  266.1 4.9 %copy.45 = bf16[1,2,1,64,16,8,128]{6,5,4,3,1,2,0:T(8,128)(2,1)S(1)} copy(bf16[1,2,1,64,16,8,128]{6,4,3,5,1,0,2:T(8,128)(2,1)S(1)} %get-tuple-element.44) | data formatting | bytes 8388608 | tf_op jit(solution)/shard_map/slice | solution.py:64
  271.0 12.0 %fusion.5 = f32[2048,2048]{1,0:T(8,128)} fusion(bf16[256,8,8,128]{3,2,1,0:T(8,128)(2,1)S(1)} %bitcast.254, bf16[1024,1024]{1,0:T(8,128)(2,1)S(1)} %copy-done.1, bf16[1024,1024]{1,0:T(8,128)(2,1)S(1)} %copy-done), kind=kOutput, calls=%fused_computation.17 | convolution fusion | flops 8598323200 | bytes 25165824 | tf_op jit(solution)/shard_map/dot_general | solution.py:69
  282.9 17.8 %convolution_add_fusion = f32[2048,2048]{1,0:T(8,128)} fusion(f32[2048,2048]{1,0:T(8,128)} %fusion.5, bf16[256,8,8,128]{3,2,1,0:T(8,128)(2,1)S(1)} %bitcast.253, bf16[1024,1024]{1,0:T(8,128)(2,1)} %get-tuple-element.46, bf16[1024,1024]{1,0:T(8,128)(2,1)S(1)} %fusion.34), kind=kOutput, calls=%fused_computation.12 | convolution fusion | flops 8602517504 | bytes 41943040 | tf_op jit(solution)/shard_map/dot_general | solution.py:69
  300.7 9.3 %fusion = f32[2048,1024]{1,0:T(8,128)} fusion(f32[2048,2048]{1,0:T(8,128)} %convolution_add_fusion), kind=kLoop, calls=%fused_computation.4 | loop fusion | flops 6291456 | bytes 25165824 | tf_op jit(solution)/shard_map/add | solution.py:74
  310.0 6.7 %reduce_sum.28 = f32[64,16,1024]{2,1,0:T(8,128)} reduce(f32[2,64,16,1024]{3,2,1,0:T(8,128)} %bitcast.250, f32[]{:T(128)} %constant.78.clone.1), dimensions={0}, to_apply=%region_1.2 | reduce | flops 1048576 | bytes 12582916 | tf_op jit(solution)/shard_map/reduce_sum | solution.py:77
  319.7 5.1 %copy.46 = bf16[32,16,1024]{0,1,2:T(8,128)(2,1)} copy(bf16[32,16,1024]{2,1,0:T(8,128)(2,1)S(1)} %multiply_convert_fusion) | data formatting | bytes 2097152 | tf_op jit(solution)/shard_map/convert_element_type | solution.py:81
  324.8 18.4 %gather_fusion = bf16[2048,32,16]{1,2,0:T(8,128)(2,1)} fusion(bf16[32,16,1024]{0,1,2:T(8,128)(2,1)} %copy.46, s32[2048]{0:T(1024)S(1)} %broadcast_clamp_fusion), kind=kCustom, calls=%fused_computation | custom fusion | bytes 4202496 | tf_op jit(solution)/shard_map/jit(_take)/gather | solution.py:94
  343.3 12.1 %fusion.39 = bf16[2048,16,32]{2,1,0:T(8,128)(2,1)} fusion(bf16[2048,32,16]{1,2,0:T(8,128)(2,1)} %gather_fusion, pred[2048]{0:T(1024)(128)(4,1)S(1)} %compare_and_fusion, pred[2048]{0:T(1024)(128)(4,1)S(1)} %fusion.20), kind=kLoop, calls=%fused_computation.176 | loop fusion | flops 2097152 | bytes 4198400
  355.3 13.4 %reshape.1023 = bf16[16,2,32768]{2,1,0:T(2,128)(2,1)S(1)} reshape(bf16[2048,16,32]{2,1,0:T(8,128)(2,1)} %fusion.39) | data formatting | bytes 4194304
  368.8 36.1 %all_to_all.33 = bf16[16,2,32768]{2,1,0:T(2,128)(2,1)} all-to-all(bf16[16,2,32768]{2,1,0:T(2,128)(2,1)S(1)} %reshape.1023), channel_id=1, replica_groups=mesh['feed'=8,'chan'=16] {'chan'}, dimensions={0} | all-to-all | bytes 4194304 | tf_op jit(solution)/shard_map/all_to_all | solution.py:97
  404.8 12.9 %reshape.1024 = bf16[2048,16,32]{2,1,0:T(8,128)(2,1)} reshape(bf16[16,2,32768]{2,1,0:T(2,128)(2,1)} %all_to_all.33) | data formatting | bytes 4194304
  417.8 11.2 %copy.48 = bf16[32,16,16,128]{3,2,1,0:T(8,128)(2,1)} copy(bf16[32,16,16,128]{0,2,3,1:T(8,128)(2,1)} %bitcast.251) | data formatting | bytes 4194304 | tf_op jit(solution)/shard_map/all_to_all | solution.py:97
  (30 shorter events, 14.5 us)
Async XLA Ops:
  80.2 5.2 %copy-start.3 = (f32[2,2,1,128]{3,2,1,0:T(1,128)S(1)}, f32[2,2,1,128]{3,2,1,0:T(1,128)}, u32[]{:S(2)}) copy-start(f32[2,2,1,128]{3,2,1,0:T(1,128)} %param.8) | copy-start | bytes 6148
  149.1 5.1 %copy-start.4 = (s32[16]{0:T(128)S(1)}, s32[16]{0:T(128)}, u32[]{:S(2)}) copy-start(s32[16]{0:T(128)} %param.11) | copy-start | bytes 196
  149.1 5.2 %copy-start.2 = (s32[16,128]{1,0:T(8,128)S(1)}, s32[16,128]{1,0:T(8,128)}, u32[]{:S(2)}) copy-start(s32[16,128]{1,0:T(8,128)} %param.10) | copy-start | bytes 24580
  149.1 99.7 %all-to-all-start = ((bf16[2,2,1,512,16,128]{5,4,1,0,2,3:T(8,128)(2,1)}), bf16[2,2,1,512,16,128]{5,4,1,0,2,3:T(8,128)(2,1)}, u32[]{:S(2)}, u32[]{:S(2)}) async-start(bf16[2,2,1,512,16,128]{5,4,1,0,2,3:T(8,128)(2,1)} %pad_maximum_fusion.1), calls=%async_computation | async-start | bytes 16777216 | tf_op jit(solution)/shard_map/all_to_all | solution.py:91
  261.2 9.8 %copy-start = (bf16[1024,1024]{1,0:T(8,128)(2,1)S(1)}, bf16[1024,1024]{1,0:T(8,128)(2,1)}, u32[]{:S(2)}) copy-start(bf16[1024,1024]{1,0:T(8,128)(2,1)} %get-tuple-element.46) | copy-start | bytes 6291460
  261.2 9.7 %copy-start.1 = (bf16[1024,1024]{1,0:T(8,128)(2,1)S(1)}, bf16[1024,1024]{1,0:T(8,128)(2,1)}, u32[]{:S(2)}) copy-start(bf16[1024,1024]{1,0:T(8,128)(2,1)} %get-tuple-element.47) | copy-start | bytes 6291460
where the time goes:
time: 438 us; the launch traced here: 429 us
  other arithmetic  158 us (36%)
  local copies, waits for them, and re-layouts  111 us (25%)
  waiting for transfers between devices  88.1 us (20%)
  blocking collectives  36.1 us (8%)
  matrix products  29.7 us (7%)
  starting transfers between devices  5.08 us (1%)
    all_to_all x1, waiting for transfers between devices, on_device(): lax.all_to_all(calibrated, 'feed', split_axis=3, concat_axis=5, tiled=True)  88.1 us
    another operation x3, other arithmetic, filterbank(): return jnp.stack([real_part, imag_part]).astype(jnp.bfloat16)  63.7 us
    add x1, other arithmetic, filterbank(): filtered + taps_window[tap_index][:, None] * frames_data[:, :, :, tap_ind...  56 us
    all_to_all x1, blocking collectives, on_device(): lax.all_to_all(jnp.where(live_slots, picked, jnp.zeros((), jnp.bfloat16))...  36.1 us
    unnamed x12, local copies, waits for them, and re-layouts  26.4 us
    gather x1, local copies, waits for them, and re-layouts, on_device(): jnp.take(detected.reshape(bins_local, coarse_local * fine_items, beam_tot...  18.4 us
    dot_general x1, matrix products, detect(): jnp.dot(rows_imag, lower_block, preferred_element_type=jnp.float32)  17.8 us
    unnamed x1, other arithmetic  12.1 us
  transfers between devices with their start and end apart: 1, of which 1 were waited for; matrix products, arithmetic and copies ran while one was open for 2% of the time, Pallas kernels for 0%

commit v1 on v0

--- a/solution.py
+++ b/solution.py
@@ -88,7 +88,10 @@
     live_slots = (jnp.arange(capacity, dtype=jnp.int32)[None, :] < beam_counts[:, None]).reshape(-1)
     stream = jnp.concatenate([history, voltages], axis=3)
     calibrated = filterbank(stream, voltages.shape[3] // U, gains)
-    beam_calibrated = lax.all_to_all(calibrated, "feed", split_axis=3, concat_axis=5, tiled=True)
+    size = lax.axis_size("feed")
+    blocks = jnp.stack(jnp.split(calibrated, size, axis=3), axis=0)
+    blocks = lax.all_to_all(blocks, "feed", split_axis=0, concat_axis=0)
+    beam_calibrated = jnp.concatenate(blocks, axis=5)
     detected = detect(beam_calibrated, weights)
     bins_local, coarse_local, fine_items, beam_total = detected.shape
     picked = jnp.take(

time: 438 us -> 389 us (0.89); the launches traced: 429 us -> 387 us
  other arithmetic: 158 us -> 123 us
  local copies, waits for them, and re-layouts: 111 us -> 104 us
    add x1, other arithmetic: 56 us -> 18.8 us  [filterbank(): filtered + taps_window[tap_index][:, None] * frames_data[:, :, :, tap_ind...]
    unnamed x1 -> x8, other arithmetic: 12.1 us -> 21.5 us
    all_to_all x1 -> x0, local copies, waits for them, and re-layouts: 8.05 us -> none  [on_device(): lax.all_to_all(calibrated, 'feed', split_axis=3, concat_axis=5, tiled=True)]
    another operation x3 -> x2, other arithmetic: 63.7 us -> 55.9 us  [filterbank(): return jnp.stack([real_part, imag_part]).astype(jnp.bfloat16)]
    unnamed x12 -> x16, local copies, waits for them, and re-layouts: 26.4 us -> 26.4 us
where the time goes in v1:
time: 389 us; the launch traced here: 387 us
  other arithmetic  123 us (32%)
  local copies, waits for them, and re-layouts  104 us (27%)
  waiting for transfers between devices  88.1 us (23%)
  blocking collectives  36.1 us (9%)
  matrix products  29.7 us (8%)
  starting transfers between devices  5.27 us (1%)
    all_to_all x1, waiting for transfers between devices, on_device(): blocks = lax.all_to_all(blocks, 'feed', split_axis=0, concat_axis=0)  88.1 us
    another operation x2, other arithmetic, filterbank(): return jnp.stack([real_part, imag_part]).astype(jnp.bfloat16)  55.9 us
    all_to_all x1, blocking collectives, on_device(): lax.all_to_all(jnp.where(live_slots, picked, jnp.zeros((), jnp.bfloat16))...  36.1 us
    unnamed x16, local copies, waits for them, and re-layouts  26.4 us
    unnamed x8, other arithmetic  21.5 us
    add x1, other arithmetic, filterbank(): filtered + taps_window[tap_index][:, None] * frames_data[:, :, :, tap_ind...  18.8 us
    gather x1, local copies, waits for them, and re-layouts, on_device(): jnp.take(detected.reshape(bins_local, coarse_local * fine_items, beam_tot...  18.4 us
    dot_general x1, matrix products, detect(): jnp.dot(rows_imag, lower_block, preferred_element_type=jnp.float32)  17.8 us
  transfers between devices with their start and end apart: 1, of which 1 were waited for; matrix products, arithmetic and copies ran while one was open for 2% of the time, Pallas kernels for 0%

profile of v1, /device:TPU:0, one launch (start us, length us, event | category | flops | bytes accessed | tf_op | source)
XLA Modules:
  0.0 387.3 jit_solution(10271877423435277908)
XLA Ops:
  0.7 4.3 %pad_maximum_fusion = bf16[2,2,1,8240,128]{4,3,2,1,0:T(8,128)(2,1)S(1)} fusion(bf16[2,2,1,8192,128]{4,3,2,1,0:T(8,128)(2,1)} %param.6, bf16[2,2,1,48,128]{4,3,2,1,0:T(8,128)(2,1)} %param.7), kind=kLoop, calls=%fused_computation.16 | loop fusion | flops 16875520 | bytes 16875520 | tf_op jit(solution)/shard_map/concatenate | solution.py:89
  5.0 11.6 %fusion.44 = (bf16[2,2,1,512,16,128]{5,4,3,1,0,2:T(8,128)(2,1)}, bf16[2,2,1,512,16,128]{5,4,3,1,0,2:T(8,128)(2,1)}, bf16[2,2,1,512,16,128]{5,4,3,1,0,2:T(8,128)(2,1)}, bf16[2,2,1,512,16,128]{5,4,3,1,0,2:T(8,128)(2,1)}) fusion(bf16[2,2,1,515,16,128]{5,4,3,1,0,2:T(8,128)(2,1)S(1)} %bitcast.265), kind=kLoop, calls=%fused_computation.202 | loop fusion | bytes 67108864 | tf_op jit(solution)/shard_map/slice | solution.py:37
  17.4 18.8 %multiply_add_fusion = f32[2,2,1,512,16,128]{5,3,1,4,2,0:T(8,128)} fusion(bf16[2,2,1,512,16,128]{5,4,3,1,0,2:T(8,128)(2,1)} %get-tuple-element.43, bf16[2,2,1,512,16,128]{5,4,3,1,0,2:T(8,128)(2,1)} %get-tuple-element.41, bf16[2,2,1,512,16,128]{5,4,3,1,0,2:T(8,128)(2,1)} %get-tuple-element.42, bf16[2,2,1,512,16,128]{5,4,3,1,0,2:T(8,128)(2,1)} %get-tuple-element.40, ...), kind=kLoop, calls=%fused_computation.1 | loop fusion | flops 46137344 | bytes 50331904 | tf_op jit(solution)/shard_map/add | solution.py:39
  36.2 6.7 %slice_bitcast_fusion.33 = (f32[2,512,128]{2,1,0:T(8,128)S(1)}, f32[2,512,128]{2,1,0:T(8,128)S(1)}, f32[2,512,128]{2,1,0:T(8,128)S(1)}, f32[2,512,128]{2,1,0:T(8...) fusion(f32[2,2,1,512,16,128]{5,3,1,4,2,0:T(8,128)} %multiply_ad, ...), kind=kLoop, calls=%fused_computation.91 | loop fusion | bytes 19922944 | tf_op jit(solution)/shard_map/mul | solution.py:48
  42.9 5.8 %slice_bitcast_fusion.32 = (f32[2,512,128]{2,1,0:T(8,128)}, f32[2,512,128]{2,1,0:T(8,128)}, f32[2,512,128]{2,1,0:T(8,128)}, f32[2,512,128]{2,1,0:T(8,128)}, f32[...) fusion(f32[2,2,1,512,16,128]{5,3,1,4,2,0:T(8,128)} %multiply_ad, ...), kind=kLoop, calls=%fused_computation.90 | loop fusion | bytes 13631488 | tf_op jit(solution)/shard_map/mul | solution.py:48
  48.9 46.9 %fusion.1 = (bf16[1,2,1,512,16,128]{5,4,3,1,0,2:T(8,128)(2,1)}, f32[1,2,512,16,128]{4,3,2,1,0:T(8,128)}, f32[1,2,512,16,128]{4,3,2,1,0:T(8,128)}) fusion(f32[2,128]{1,0:T(2,128)S(1)} %bitcast.274, f32[2,128]{1,0:T(2,128)S(1)} %bitcast.272, f32[16]{0:T(128)S(1)} %get-tuple-element.81, f32[2,512,128]{2,1,0:T(8,128)S(1)} %get-tuple-element.9, ...), kind=kLoop, calls=%fused_computation.26 | loop fusion | flops 272629760 | bytes 37754880 | tf_op jit(solution)/shard_map/stack | solution.py:56
  95.8 9.0 %fusion.2 = bf16[1,2,1,512,16,128]{5,4,3,1,0,2:T(8,128)(2,1)} fusion(f32[1,2,512,16,128]{4,3,2,1,0:T(8,128)} %get-tuple-element.7, f32[1,2,512,16,128]{4,3,2,1,0:T(8,128)} %get-tuple-element.6, f32[2,128]{1,0:T(2,128)S(1)} %bitcast.275, f32[2,128]{1,0:T(2,128)S(1)} %bitcast.273), kind=kLoop, calls=%fused_computation.27 | loop fusion | flops 8388608 | bytes 20973568 | tf_op jit(solution)/shard_map/stack | solution.py:56
  115.4 5.3 %all-to-all-start = ((bf16[8,2,2,1,64,16,128]{6,5,4,2,1,3,0:T(8,128)(2,1)}), bf16[8,2,2,1,64,16,128]{6,5,4,2,1,3,0:T(8,128)(2,1)}, u32[]{:S(2)}, u32[]{:S(2)}) async-start(bf16[8,2,2,1,64,16,128]{6,5,4,2,1,3,0:T(8,128)(2,1)} %fusion.22), calls=%async_computation | async-start | bytes 16777216 | tf_op jit(solution)/shard_map/all_to_all | solution.py:93
  122.6 4.7 %slice_bitcast_fusion.1 = (bf16[1024,1024]{1,0:T(8,128)(2,1)}, bf16[1024,1024]{1,0:T(8,128)(2,1)}) fusion(bf16[2,1,1024,1024]{3,2,1,0:T(8,128)(2,1)} %param.9), kind=kLoop, calls=%fused_computation.42 | loop fusion | bytes 8388608 | tf_op jit(solution)/shard_map/squeeze | solution.py:65
  127.3 88.1 %all-to-all-done = bf16[8,2,2,1,64,16,128]{6,5,4,2,1,3,0:T(8,128)(2,1)} async-done(((bf16[8,2,2,1,64,16,128]{6,5,4,2,1,3,0:T(8,128)(2,1)}), bf16[8,2,2,1,64,16,128]{6,5,4,2,1,3,0:T(8,128)(2,1)}, u32[]{:S(2)}, u32[]{:S(2)}) %all-to-all-start) | async-done | bytes 8388640 | tf_op jit(solution)/shard_map/all_to_all | solution.py:93
  215.3 4.3 %fusion.45 = (bf16[1,2,1,64,16,8,128]{6,4,3,1,0,2,5:T(8,128)(2,1)S(1)}, bf16[1,2,1,64,16,8,128]{6,4,3,1,0,2,5:T(8,128)(2,1)S(1)}) fusion(bf16[2,2,1,64,16,8,128]{6,4,3,1,0,2,5:T(8,128)(2,1)} %bitcast.114), kind=kLoop, calls=%fused_computation.203 | loop fusion | bytes 16777216 | tf_op jit(solution)/shard_map/slice | solution.py:64
  219.6 4.9 %copy.47 = bf16[1,2,1,64,16,8,128]{6,5,4,3,1,2,0:T(8,128)(2,1)S(1)} copy(bf16[1,2,1,64,16,8,128]{6,4,3,1,0,2,5:T(8,128)(2,1)S(1)} %get-tuple-element.45) | data formatting | bytes 8388608 | tf_op jit(solution)/shard_map/slice | solution.py:63
  224.5 4.9 %copy.48 = bf16[1,2,1,64,16,8,128]{6,5,4,3,1,2,0:T(8,128)(2,1)S(1)} copy(bf16[1,2,1,64,16,8,128]{6,4,3,1,0,2,5:T(8,128)(2,1)S(1)} %get-tuple-element.44) | data formatting | bytes 8388608 | tf_op jit(solution)/shard_map/slice | solution.py:64
  229.4 12.0 %fusion.5 = f32[2048,2048]{1,0:T(8,128)} fusion(bf16[256,8,8,128]{3,2,1,0:T(8,128)(2,1)S(1)} %bitcast.269, bf16[1024,1024]{1,0:T(8,128)(2,1)S(1)} %copy-done.3, bf16[1024,1024]{1,0:T(8,128)(2,1)S(1)} %copy-done.2), kind=kOutput, calls=%fused_computation.30 | convolution fusion | flops 8598323200 | bytes 25165824 | tf_op jit(solution)/shard_map/dot_general | solution.py:69
  241.3 17.8 %convolution_add_fusion = f32[2048,2048]{1,0:T(8,128)} fusion(f32[2048,2048]{1,0:T(8,128)} %fusion.5, bf16[256,8,8,128]{3,2,1,0:T(8,128)(2,1)S(1)} %bitcast.268, bf16[1024,1024]{1,0:T(8,128)(2,1)} %get-tuple-element.46, bf16[1024,1024]{1,0:T(8,128)(2,1)S(1)} %fusion.43), kind=kOutput, calls=%fused_computation.25 | convolution fusion | flops 8602517504 | bytes 41943040 | tf_op jit(solution)/shard_map/dot_general | solution.py:69
  259.1 9.3 %fusion = f32[2048,1024]{1,0:T(8,128)} fusion(f32[2048,2048]{1,0:T(8,128)} %convolution_add_fusion), kind=kLoop, calls=%fused_computation.18 | loop fusion | flops 6291456 | bytes 25165824 | tf_op jit(solution)/shard_map/add | solution.py:74
  268.4 6.7 %reduce_sum.28 = f32[64,16,1024]{2,1,0:T(8,128)} reduce(f32[2,64,16,1024]{3,2,1,0:T(8,128)} %bitcast.266, f32[]{:T(128)} %constant.78.clone.1), dimensions={0}, to_apply=%region_1.2 | reduce | flops 1048576 | bytes 12582916 | tf_op jit(solution)/shard_map/reduce_sum | solution.py:77
  278.1 5.2 %copy.49 = bf16[32,16,1024]{0,1,2:T(8,128)(2,1)} copy(bf16[32,16,1024]{2,1,0:T(8,128)(2,1)S(1)} %multiply_convert_fusion) | data formatting | bytes 2097152 | tf_op jit(solution)/shard_map/convert_element_type | solution.py:81
  283.3 18.4 %gather_fusion = bf16[2048,32,16]{1,2,0:T(8,128)(2,1)} fusion(bf16[32,16,1024]{0,1,2:T(8,128)(2,1)} %copy.49, s32[2048]{0:T(1024)S(1)} %broadcast_clamp_fusion), kind=kCustom, calls=%fused_computation | custom fusion | bytes 4202496 | tf_op jit(solution)/shard_map/jit(_take)/gather | solution.py:97
  301.6 12.1 %fusion.48 = bf16[2048,16,32]{2,1,0:T(8,128)(2,1)} fusion(bf16[2048,32,16]{1,2,0:T(8,128)(2,1)} %gather_fusion, pred[2048]{0:T(1024)(128)(4,1)S(1)} %compare_and_fusion, pred[2048]{0:T(1024)(128)(4,1)S(1)} %fusion.29), kind=kLoop, calls=%fused_computation.206 | loop fusion | flops 2097152 | bytes 4198400
  313.7 13.4 %reshape.1028 = bf16[16,2,32768]{2,1,0:T(2,128)(2,1)S(1)} reshape(bf16[2048,16,32]{2,1,0:T(8,128)(2,1)} %fusion.48) | data formatting | bytes 4194304
  327.1 36.1 %all_to_all.23 = bf16[16,2,32768]{2,1,0:T(2,128)(2,1)} all-to-all(bf16[16,2,32768]{2,1,0:T(2,128)(2,1)S(1)} %reshape.1028), channel_id=1, replica_groups=mesh['feed'=8,'chan'=16] {'chan'}, dimensions={0} | all-to-all | bytes 4194304 | tf_op jit(solution)/shard_map/all_to_all | solution.py:100
  363.2 12.9 %reshape.1029 = bf16[2048,16,32]{2,1,0:T(8,128)(2,1)} reshape(bf16[16,2,32768]{2,1,0:T(2,128)(2,1)} %all_to_all.23) | data formatting | bytes 4194304
  376.1 11.2 %copy.51 = bf16[32,16,16,128]{3,2,1,0:T(8,128)(2,1)} copy(bf16[32,16,16,128]{0,2,3,1:T(8,128)(2,1)} %bitcast.267) | data formatting | bytes 4194304 | tf_op jit(solution)/shard_map/all_to_all | solution.py:100
  (40 shorter events, 16.5 us)
Async XLA Ops:
  42.9 6.0 %copy-start.5 = (f32[2,2,1,128]{3,2,1,0:T(1,128)S(1)}, f32[2,2,1,128]{3,2,1,0:T(1,128)}, u32[]{:S(2)}) copy-start(f32[2,2,1,128]{3,2,1,0:T(1,128)} %param.8) | copy-start | bytes 6148
  95.7 9.1 %copy-start = (bf16[1,2,1,512,16,128]{5,4,3,1,0,2:T(8,128)(2,1)S(1)}, bf16[1,2,1,512,16,128]{5,4,3,1,0,2:T(8,128)(2,1)}, u32[]{:S(2)}) copy-start(bf16[1,2,1,512,16,128]{5,4,3,1,0,2:T(8,128)(2,1)} %get-tuple-element.5) | copy-start | bytes 12582916
  104.8 2.4 copy-start.1
  115.4 5.3 %copy-start.6 = (s32[16]{0:T(128)S(1)}, s32[16]{0:T(128)}, u32[]{:S(2)}) copy-start(s32[16]{0:T(128)} %param.11) | copy-start | bytes 196
  115.4 5.4 %copy-start.4 = (s32[16,128]{1,0:T(8,128)S(1)}, s32[16,128]{1,0:T(8,128)}, u32[]{:S(2)}) copy-start(s32[16,128]{1,0:T(8,128)} %param.10) | copy-start | bytes 24580
  115.4 99.9 %all-to-all-start = ((bf16[8,2,2,1,64,16,128]{6,5,4,2,1,3,0:T(8,128)(2,1)}), bf16[8,2,2,1,64,16,128]{6,5,4,2,1,3,0:T(8,128)(2,1)}, u32[]{:S(2)}, u32[]{:S(2)}) async-start(bf16[8,2,2,1,64,16,128]{6,5,4,2,1,3,0:T(8,128)(2,1)} %fusion.22), calls=%async_computation | async-start | bytes 16777216 | tf_op jit(solution)/shard_map/all_to_all | solution.py:93
  219.6 9.8 %copy-start.2 = (bf16[1024,1024]{1,0:T(8,128)(2,1)S(1)}, bf16[1024,1024]{1,0:T(8,128)(2,1)}, u32[]{:S(2)}) copy-start(bf16[1024,1024]{1,0:T(8,128)(2,1)} %get-tuple-element.46) | copy-start | bytes 6291460
  219.6 9.7 %copy-start.3 = (bf16[1024,1024]{1,0:T(8,128)(2,1)S(1)}, bf16[1024,1024]{1,0:T(8,128)(2,1)}, u32[]{:S(2)}) copy-start(bf16[1024,1024]{1,0:T(8,128)(2,1)} %get-tuple-element.47) | copy-start | bytes 6291460
